TPU v7x, 512 devices: a whole 4x4x16 slice. The times are simulated.
512 devices in a mesh: grp: 16 (over x, y), clu: 32 (over z, core).
Axes of the slice: x: 4, y: 4, z: 16, core: 2. Of those that a mesh axis runs over, the one named last changes fastest.
Arguments:
- lower_inverse: bfloat16 [32, 2, 512, 512], P('clu', None, 'grp'), as said below
- upper_inverse: bfloat16 [32, 2, 512, 512], P('clu', None, 'grp'), as said below
- lower_factors: bfloat16 [32, 128, 2, 48, 512], P('clu', 'grp'), may hold values from -1.2578125 to 1.2578125
- upper_factors: bfloat16 [32, 128, 2, 48, 512], P('clu', 'grp'), may hold values from -1.2578125 to 1.2578125
- lower_ranks: int32 [32, 128], P('clu', 'grp'), may hold values from 16 to 48
- upper_ranks: int32 [32, 128], P('clu', 'grp'), may hold values from 16 to 48
- pivots: int32 [32, 512], P('clu'), may hold values from 0 to 511, each once within a row
- pair_lower: int32 [32, 512], P('clu', 'grp'), may hold values from 0 to 7
- pair_upper: int32 [32, 512], P('clu', 'grp'), may hold values from 0 to 7
- pair_owner: int32 [32, 512, 1], P('clu', 'grp'), may hold values from 0 to 31; in each aligned block of 32 rows (0 to 31, 32 to 63, ..., all dimensions but the last counted through in order) at most 2 rows name the same one
Outputs:
- lower_solved: bfloat16 [32, 128, 2, 48, 512], P('clu', 'grp')
- upper_solved: bfloat16 [32, 128, 2, 48, 512], P('clu', 'grp')
- arrived: bfloat16 [32, 16, 32, 2, 2, 2304], P('clu', 'grp')
Inputs may be any that keep to these rules, and one draw needn't show every extreme that they name: `lower_inverse`: each cluster's matrix is unit lower triangular: zeros above the diagonal, one on the real part's diagonal and zero on the imaginary part's. `upper_inverse`: each cluster's matrix is upper triangular: zeros below the diagonal in both parts. `pair_owner`: among the 32 pairs of one share, at most 2 name the same owner, and some share reaches it.
All inputs are finite; a program needn't handle non-finite values.
Results may differ from a plain program's by a relative error of at most 0.0058.
Values may be sent and summed in bfloat16 or wider, within the bound.
No kernel may reach another device: no remote copies, remote signals or barrier semaphores. Data moves between devices by JAX's collectives and lax.ppermute only.
A program may use at most 64 MiB of HBM per device.

v0:
```python
import jax
import jax.numpy as jnp
from jax import lax
from jax.sharding import PartitionSpec as P

SEND_CAP = 2


def mask_rows(factors, block_ranks):
    rank_width = factors.shape[2]
    row_index = lax.broadcasted_iota(jnp.int32, (factors.shape[0], rank_width), 1)
    row_mask = row_index < block_ranks[:, None]
    return jnp.where(row_mask[:, None, :, None], factors, jnp.zeros((), factors.dtype))


def product(left, right):
    return jnp.einsum("prb,psb->prs", left, right, preferred_element_type=jnp.float32)


def per_device(
    lower_inverse,
    upper_inverse,
    lower_factors,
    upper_factors,
    lower_ranks,
    upper_ranks,
    pivots,
    pair_lower,
    pair_upper,
    pair_owner,
):
    lower_masked = mask_rows(lower_factors[0], lower_ranks[0])
    upper_masked = mask_rows(upper_factors[0], upper_ranks[0])
    upper_pivoted = jnp.take(upper_masked, pivots[0], axis=3)
    block_count = lower_masked.shape[0]
    rank_width = lower_masked.shape[2]
    panel_count = lower_masked.shape[3]
    lower_real = lower_masked[:, 0].reshape(block_count * rank_width, panel_count)
    lower_imag = lower_masked[:, 1].reshape(block_count * rank_width, panel_count)
    upper_real = upper_pivoted[:, 0].reshape(block_count * rank_width, panel_count)
    upper_imag = upper_pivoted[:, 1].reshape(block_count * rank_width, panel_count)
    contract_last = (((1,), (1,)), ((), ()))
    lower_piece = lax.all_gather(lower_inverse, "grp", axis=2, tiled=True)
    upper_piece = lax.all_gather(upper_inverse, "grp", axis=2, tiled=True)
    piece_real = upper_piece[0, 0]
    piece_imag = upper_piece[0, 1]
    real_part = jnp.dot(lower_real, piece_real, preferred_element_type=jnp.float32) - jnp.dot(
        lower_imag, piece_imag, preferred_element_type=jnp.float32
    )
    imag_part = jnp.dot(lower_real, piece_imag, preferred_element_type=jnp.float32) + jnp.dot(
        lower_imag, piece_real, preferred_element_type=jnp.float32
    )
    lower_totals = jnp.stack([real_part, imag_part], 0)
    piece_real = lower_piece[0, 0]
    piece_imag = lower_piece[0, 1]
    real_part = lax.dot_general(
        upper_real, piece_real, contract_last, preferred_element_type=jnp.float32
    ) - lax.dot_general(upper_imag, piece_imag, contract_last, preferred_element_type=jnp.float32)
    imag_part = lax.dot_general(
        upper_real, piece_imag, contract_last, preferred_element_type=jnp.float32
    ) + lax.dot_general(upper_imag, piece_real, contract_last, preferred_element_type=jnp.float32)
    upper_totals = jnp.stack([real_part, imag_part], 0)
    lower_solved = jnp.transpose(
        lower_totals.astype(jnp.bfloat16).reshape(2, block_count, rank_width, panel_count),
        (1, 0, 2, 3),
    )
    upper_solved = jnp.transpose(
        upper_totals.astype(jnp.bfloat16).reshape(2, block_count, rank_width, panel_count),
        (1, 0, 2, 3),
    )
    left_blocks = lower_solved[pair_lower[0]]
    right_blocks = upper_solved[pair_upper[0]]
    pair_count = left_blocks.shape[0]
    real_part = product(left_blocks[:, 0], right_blocks[:, 0]) - product(
        left_blocks[:, 1], right_blocks[:, 1]
    )
    imag_part = product(left_blocks[:, 0], right_blocks[:, 1]) + product(
        left_blocks[:, 1], right_blocks[:, 0]
    )
    cores = (
        jnp.stack([real_part, imag_part], 1)
        .reshape(pair_count, 2 * rank_width * rank_width)
        .astype(jnp.bfloat16)
    )
    owners = pair_owner[0, :, 0]
    pair_ids = lax.broadcasted_iota(jnp.int32, (pair_count,), 0)
    same_owner = (owners[:, None] == owners[None, :]) & (pair_ids[None, :] < pair_ids[:, None])
    slots = jnp.sum(same_owner.astype(jnp.int32), axis=1)
    clusters = lax.axis_size("clu")
    target_slot = owners * SEND_CAP + slots
    slot_ids = lax.broadcasted_iota(jnp.int32, (clusters * SEND_CAP, pair_count), 0)
    one_hot = (slot_ids == target_slot[None, :]).astype(jnp.bfloat16)
    buffer = jnp.dot(one_hot, cores, preferred_element_type=jnp.float32).astype(jnp.bfloat16)
    buffer = buffer.reshape(clusters, SEND_CAP, 2, rank_width * rank_width)
    arrived = lax.all_to_all(buffer, "clu", split_axis=0, concat_axis=0, tiled=True)
    return (lower_solved[None], upper_solved[None], arrived[None, None])


def solution(mesh):
    in_specs = (
        P("clu", None, "grp", None),
        P("clu", None, "grp", None),
        P("clu", "grp", None, None, None),
        P("clu", "grp", None, None, None),
        P("clu", "grp"),
        P("clu", "grp"),
        P("clu", None),
        P("clu", "grp"),
        P("clu", "grp"),
        P("clu", "grp", None),
    )
    out_specs = (
        P("clu", "grp", None, None, None),
        P("clu", "grp", None, None, None),
        P("clu", "grp", None, None, None, None),
    )
    return jax.shard_map(
        per_device, mesh=mesh, in_specs=in_specs, out_specs=out_specs, check_vma=False
    )
```

profile of v0, /device:TPU:1, one launch (start us, length us, event | category | flops | bytes accessed | tf_op | source)
XLA Modules:
  0.0 210.7 jit_solution(4374763556248300210)
XLA Ops:
  8.7 2.6 %copy.48 = bf16[1,8,2,48,512]{3,1,4,2,0:T(8,128)(2,1)S(1)} copy(bf16[1,8,2,48,512]{4,3,2,1,0:T(8,128)(2,1)} %param.13) | data formatting | bytes 1572864 | tf_op args[3]
  11.4 2.5 %copy.43 = bf16[1,8,2,48,512]{3,1,4,2,0:T(8,128)(2,1)} copy(bf16[1,8,2,48,512]{4,3,2,1,0:T(8,128)(2,1)S(1)} %copy-done.8) | data formatting | bytes 1572864 | tf_op args[2]
  14.0 1.4 bitcast_select_fusion
  15.4 3.0 %gather_fusion = bf16[512,8,2,48]{3,1,2,0:T(8,128)(2,1)S(1)} fusion(bf16[8,2,48,512]{2,0,3,1:T(8,128)(2,1)} %bitcast_select_fusion, s32[1024]{0:T(1024)S(1)} %pad_clamp_fusion.2), kind=kCustom, calls=%fused_computation | custom fusion | bytes 1574912 | tf_op jit(solution)/shard_map/jit(_take)/gather | solution.py:34
  18.4 1.8 select_bitcast_fusion
  20.3 1.1 fusion.26
  21.4 2.6 %copy.49 = bf16[8,1,48,512]{3,2,0,1:T(8,128)(2,1)} copy(bf16[8,1,48,512]{2,0,1,3:T(8,128)(2,1)} %get-tuple-element.4) | data formatting | bytes 786432 | tf_op jit(solution)/shard_map/slice | solution.py:40
  24.0 0.7 copy.50
  24.8 1.1 fusion.27
  25.9 2.7 %copy.44 = bf16[8,1,48,512]{3,2,0,1:T(8,128)(2,1)} copy(bf16[8,1,48,512]{2,0,3,1:T(8,128)(2,1)} %get-tuple-element.6) | data formatting | bytes 786432 | tf_op jit(solution)/shard_map/slice | solution.py:38
  29.5 42.9 %all-gather.5.cloned.1.call-done = bf16[1,2,512,512]{3,2,1,0:T(8,128)(2,1)} async-done(((bf16[1,2,32,512]{3,2,1,0:T(8,128)(2,1)}), bf16[1,2,512,512]{3,2,1,0:T(8,128)(2,1)}) %all-gather.5.cloned.1.call-update) | async-done | bytes 1048592 | tf_op jit(solution)/shard_map/all_gather | solution.py:43
  72.4 2.3 %fusion.21 = f32[384,512]{1,0:T(8,128)} fusion(bf16[384,512]{1,0:T(8,128)(2,1)S(1)} %bitcast.132, bf16[1,2,512,512]{3,2,1,0:T(8,128)(2,1)} %all-gather.5.cloned.1.call-done), kind=kOutput, calls=%fused_computation.43 | convolution fusion | flops 201326592 | bytes 1703936 | tf_op jit(solution)/shard_map/dot_general | solution.py:59
  74.7 1.4 fusion.20
  76.2 56.5 %all-gather.3.cloned.1.call-done = bf16[1,2,512,512]{3,2,1,0:T(8,128)(2,1)} async-done(((bf16[1,2,32,512]{3,2,1,0:T(8,128)(2,1)}), bf16[1,2,512,512]{3,2,1,0:T(8,128)(2,1)}) %all-gather.3.cloned.1.call-update) | async-done | bytes 1048592 | tf_op jit(solution)/shard_map/all_gather | solution.py:44
  132.7 1.5 fusion.19
  134.2 1.4 fusion.18
  137.6 1.3 fusion.15
  138.9 2.4 %gather_fusion.1 = bf16[32,2,48,512]{3,2,1,0:T(8,128)(2,1)} fusion(bf16[8,2,48,512]{3,2,1,0:T(8,128)(2,1)S(1)} %get-tuple-element.12, s32[1024]{0:T(1024)S(1)} %pad_clamp_fusion.1), kind=kCustom, calls=%fused_computation.1 | custom fusion | bytes 6291584 | tf_op jit(solution)/shard_map/gather | solution.py:71
  141.3 2.4 %gather_fusion.2 = bf16[32,2,48,512]{3,2,1,0:T(8,128)(2,1)} fusion(bf16[8,2,48,512]{3,2,1,0:T(8,128)(2,1)S(1)} %get-tuple-element.7, s32[1024]{0:T(1024)S(1)} %pad_clamp_fusion), kind=kCustom, calls=%fused_computation.2 | custom fusion | bytes 6291584 | tf_op jit(solution)/shard_map/gather | solution.py:72
  143.8 2.6 %fusion = f32[32,48,48]{2,1,0:T(8,128)S(1)} fusion(bf16[32,2,48,512]{3,2,1,0:T(8,128)(2,1)} %gather_fusion.1, bf16[32,2,48,512]{3,2,1,0:T(8,128)(2,1)} %gather_fusion.2), kind=kOutput, calls=%fused_computation.11 | convolution fusion | flops 75497472 | bytes 3440640 | tf_op jit(solution)/shard_map/prb,psb->prs/dot_general | solution.py:17
  146.6 2.1 fusion.1
  150.3 1.4 convert_element_type.16
  152.2 50.9 %all_to_all.5 = bf16[32,2,2,2304]{3,2,1,0:T(2,128)(2,1)S(1)} all-to-all(bf16[32,2,2,2304]{3,2,1,0:T(2,128)(2,1)S(1)} %reshape.167), channel_id=1, replica_groups=mesh['grp'=16,'clu'=32] {'clu'}, dimensions={0} | all-to-all | bytes 1179648 | tf_op jit(solution)/shard_map/all_to_all | solution.py:95
  203.0 0.8 copy.63
  (57 shorter events, 7.0 us)
Async XLA Ops:
  7.2 4.1 %copy-start.10 = (s32[1,8]{1,0:T(1,128)S(1)}, s32[1,8]{1,0:T(1,128)}, u32[]{:S(2)}) copy-start(s32[1,8]{1,0:T(1,128)} %param.15) | copy-start | bytes 100
  7.2 4.2 %copy-start.9 = (s32[1,512]{1,0:T(1,128)S(1)}, s32[1,512]{1,0:T(1,128)}, u32[]{:S(2)}) copy-start(s32[1,512]{1,0:T(1,128)} %param.16) | copy-start | bytes 6148
  7.2 4.2 %copy-start.8 = (bf16[1,8,2,48,512]{4,3,2,1,0:T(8,128)(2,1)S(1)}, bf16[1,8,2,48,512]{4,3,2,1,0:T(8,128)(2,1)}, u32[]{:S(2)}) copy-start(bf16[1,8,2,48,512]{4,3,2,1,0:T(8,128)(2,1)} %param.12) | copy-start | bytes 2359300
  7.2 65.2 %all-gather.5.cloned.1.call-start = ((), (), s32[]{:S(2)}) async-start(), calls=%async_computation.2 | async-start | bytes 1114112 | tf_op jit(solution)/shard_map/all_gather | solution.py:43
  7.9 124.8 %all-gather.3.cloned.1.call-start = ((), (), s32[]{:S(2)}) async-start(), calls=%async_computation.1 | async-start | bytes 1114112 | tf_op jit(solution)/shard_map/all_gather | solution.py:44
  11.3 2.6 %copy-start.11 = (s32[1,8]{1,0:T(1,128)S(1)}, s32[1,8]{1,0:T(1,128)}, u32[]{:S(2)}) copy-start(s32[1,8]{1,0:T(1,128)} %param.14) | copy-start | bytes 100
  18.4 1.8 copy-start
  25.9 3.4 %copy-start.12 = (s32[1,32]{1,0:T(1,128)S(1)}, s32[1,32]{1,0:T(1,128)}, u32[]{:S(2)}) copy-start(s32[1,32]{1,0:T(1,128)} %param.17) | copy-start | bytes 388
  25.9 3.4 %copy-start.13 = (s32[1,32]{1,0:T(1,128)S(1)}, s32[1,32]{1,0:T(1,128)}, u32[]{:S(2)}) copy-start(s32[1,32]{1,0:T(1,128)} %param.18) | copy-start | bytes 388
  25.9 3.5 %copy-start.14 = (s32[1,32,1]{1,2,0:T(1,128)S(1)}, s32[1,32,1]{1,2,0:T(1,128)}, u32[]{:S(2)}) copy-start(s32[1,32,1]{1,2,0:T(1,128)} %param.19) | copy-start | bytes 388
  25.9 46.5 %copy-start.3 = (bf16[8,1,48,512]{3,2,0,1:T(8,128)(2,1)S(1)}, bf16[8,1,48,512]{3,2,0,1:T(8,128)(2,1)}, u32[]{:S(2)}) copy-start(bf16[8,1,48,512]{3,2,0,1:T(8,128)(2,1)} %copy.49) | copy-start | bytes 1179652
  29.3 103.4 %copy-start.4 = (bf16[8,1,48,512]{3,2,0,1:T(8,128)(2,1)S(1)}, bf16[8,1,48,512]{3,2,0,1:T(8,128)(2,1)}, u32[]{:S(2)}) copy-start(bf16[8,1,48,512]{3,2,0,1:T(8,128)(2,1)} %copy.44) | copy-start | bytes 1179652
  76.2 59.4 %copy-start.1 = (bf16[1,2,512,512]{3,2,1,0:T(8,128)(2,1)S(1)}, bf16[1,2,512,512]{3,2,1,0:T(8,128)(2,1)}, u32[]{:S(2)}) copy-start(bf16[1,2,512,512]{3,2,1,0:T(8,128)(2,1)} %all-gather.5.cloned.1.call-done) | copy-start | bytes 3145732
  132.7 2.9 %copy-start.7 = (f32[384,512]{1,0:T(8,128)S(1)}, f32[384,512]{1,0:T(8,128)}, u32[]{:S(2)}) copy-start(f32[384,512]{1,0:T(8,128)} %fusion.21) | copy-start | bytes 2359300
  135.6 1.2 copy-start.2
  143.8 2.8 %copy-start.5 = (bf16[32,2,48,512]{3,2,1,0:T(8,128)(2,1)S(1)}, bf16[32,2,48,512]{3,2,1,0:T(8,128)(2,1)}, u32[]{:S(2)}) copy-start(bf16[32,2,48,512]{3,2,1,0:T(8,128)(2,1)} %gather_fusion.1) | copy-start | bytes 9437188
  146.6 2.4 %copy-start.6 = (bf16[32,2,48,512]{3,2,1,0:T(8,128)(2,1)S(1)}, bf16[32,2,48,512]{3,2,1,0:T(8,128)(2,1)}, u32[]{:S(2)}) copy-start(bf16[32,2,48,512]{3,2,1,0:T(8,128)(2,1)} %gather_fusion.2) | copy-start | bytes 9437188
Sparse Core Ops, SparseCore 0:
  11.1 61.2 all-gather.4
  75.5 57.1 all-gather.2
where the time goes:
time: 211 us
  waiting for transfers between devices  101 us (48%)
  blocking collectives  50.9 us (24%)
  local copies, waits for them, and re-layouts  25.2 us (12%)
  between operations  14.4 us (7%)
  matrix products  14.2 us (7%)
  other arithmetic  5.23 us (2%)
    all_gather x1, waiting for transfers between devices, per_device(): upper_piece = lax.all_gather(upper_inverse, 'grp', axis=2, tiled=True)  56.5 us
    all_to_all x1, blocking collectives, per_device(): lax.all_to_all(buffer, 'clu', split_axis=0, concat_axis=0, tiled=True)  50.9 us
    all_gather x1, waiting for transfers between devices, per_device(): lower_piece = lax.all_gather(lower_inverse, 'grp', axis=2, tiled=True)  42.9 us
    unnamed x33, local copies, waits for them, and re-layouts  6.88 us
    dot_general x4, matrix products, product(): jnp.einsum('prb,psb->prs', left, right, preferred_element_type=jnp.float32)  5.78 us
  transfers between devices with their start and end apart: 2, of which 2 were waited for; matrix products, arithmetic and copies ran while one was open for 12% of the time, Pallas kernels for 0%

commit v1 on v0

--- a/solution.py
+++ b/solution.py
@@ -29,6 +29,16 @@
     pair_upper,
     pair_owner,
 ):
+
+    def fill_the_matrix(message, on_dim):
+        carry_in = jnp.concatenate(
+            lax.all_to_all(
+                jnp.stack(tuple((message for _ in range(lax.axis_size("grp")))), 0), "grp", 0, 0
+            ),
+            axis=on_dim,
+        )
+        return carry_in
+
     lower_masked = mask_rows(lower_factors[0], lower_ranks[0])
     upper_masked = mask_rows(upper_factors[0], upper_ranks[0])
     upper_pivoted = jnp.take(upper_masked, pivots[0], axis=3)
@@ -40,7 +50,7 @@
     upper_real = upper_pivoted[:, 0].reshape(block_count * rank_width, panel_count)
     upper_imag = upper_pivoted[:, 1].reshape(block_count * rank_width, panel_count)
     contract_last = (((1,), (1,)), ((), ()))
-    lower_piece = lax.all_gather(lower_inverse, "grp", axis=2, tiled=True)
+    lower_piece = fill_the_matrix(lower_inverse, 2)
     upper_piece = lax.all_gather(upper_inverse, "grp", axis=2, tiled=True)
     piece_real = upper_piece[0, 0]
     piece_imag = upper_piece[0, 1]

time: 211 us -> 159 us (0.75)
  waiting for transfers between devices: 101 us -> 41.8 us
  starting transfers between devices: 0.08 us -> 7.75 us
  matrix products: 14.2 us -> 12 us
    all_gather x1 -> x0, waiting for transfers between devices: 42.9 us -> none  [per_device(): lower_piece = lax.all_gather(lower_inverse, 'grp', axis=2, tiled=True)]
    all_gather x1, waiting for transfers between devices: 56.5 us -> 41.1 us  [per_device(): upper_piece = lax.all_gather(upper_inverse, 'grp', axis=2, tiled=True)]
    all_to_all x0 -> x1, starting transfers between devices: none -> 7.7 us  [fill_the_matrix(): lax.all_to_all(jnp.stack(tuple((message for _ in range(lax.axis_size('grp...]
    unnamed x33 -> x31, local copies, waits for them, and re-layouts: 6.88 us -> 7.54 us
  transfers between devices with their start and end apart: 2 -> 2, of which waited for: 2 -> 1; matrix products, arithmetic and copies ran while one was open for 12% -> 14% of each run, Pallas kernels for 0% -> 0%
where the time goes in v1:
time: 159 us
  blocking collectives  50.9 us (32%)
  waiting for transfers between devices  41.8 us (26%)
  local copies, waits for them, and re-layouts  26.7 us (17%)
  between operations  14.3 us (9%)
  matrix products  12 us (8%)
  starting transfers between devices  7.75 us (5%)
  other arithmetic  5.27 us (3%)
    all_to_all x1, blocking collectives, per_device(): lax.all_to_all(buffer, 'clu', split_axis=0, concat_axis=0, tiled=True)  50.9 us
    all_gather x1, waiting for transfers between devices, per_device(): upper_piece = lax.all_gather(upper_inverse, 'grp', axis=2, tiled=True)  41.1 us
    all_to_all x1, starting transfers between devices, fill_the_matrix(): lax.all_to_all(jnp.stack(tuple((message for _ in range(lax.axis_size('grp...  7.7 us
    unnamed x31, local copies, waits for them, and re-layouts  7.54 us
    dot_general x4, matrix products, product(): jnp.einsum('prb,psb->prs', left, right, preferred_element_type=jnp.float32)  5.78 us
  transfers between devices with their start and end apart: 2, of which 1 were waited for; matrix products, arithmetic and copies ran while one was open for 14% of the time, Pallas kernels for 0%

profile of v1, /device:TPU:1, one launch (start us, length us, event | category | flops | bytes accessed | tf_op | source)
XLA Modules:
  0.0 158.7 jit_solution(6042817532090530285)
XLA Ops:
  7.2 2.0 %stack.52 = bf16[16,1,2,32,512]{4,3,2,1,0:T(8,128)(2,1)} broadcast(bf16[2,32,512]{2,1,0:T(8,128)(2,1)} %bitcast.149), dimensions={2,3,4} | broadcast | bytes 1114112 | tf_op jit(solution)/shard_map/stack | solution.py:36
  9.1 7.7 %all-to-all-start = ((bf16[16,1,2,32,512]{4,3,2,1,0:T(8,128)(2,1)}), bf16[16,1,2,32,512]{4,3,2,1,0:T(8,128)(2,1)S(1)}, u32[]{:S(2)}, u32[]{:S(2)}) async-start(bf16[16,1,2,32,512]{4,3,2,1,0:T(8,128)(2,1)} %stack.52), calls=%async_computation | async-start | bytes 2097152 | tf_op jit(solution)/shard_map/all_to_all | solution.py:35
  17.6 2.6 %copy.64 = bf16[1,8,2,48,512]{3,1,4,2,0:T(8,128)(2,1)S(1)} copy(bf16[1,8,2,48,512]{4,3,2,1,0:T(8,128)(2,1)} %param.13) | data formatting | bytes 1572864 | tf_op args[3]
  20.3 1.5 bitcast_select_fusion
  21.8 3.0 %gather_fusion = bf16[512,8,2,48]{3,1,2,0:T(8,128)(2,1)S(1)} fusion(bf16[8,2,48,512]{2,0,3,1:T(8,128)(2,1)} %bitcast_select_fusion, s32[1024]{0:T(1024)S(1)} %pad_clamp_fusion.2), kind=kCustom, calls=%fused_computation | custom fusion | bytes 1574912 | tf_op jit(solution)/shard_map/jit(_take)/gather | solution.py:44
  24.7 1.8 %select_bitcast_fusion = bf16[8,2,48,512]{2,0,1,3:T(8,128)(2,1)S(1)} fusion(bf16[512,8,2,48]{3,1,2,0:T(8,128)(2,1)S(1)} %gather_fusion, pred[512]{0:T(512)(128)(4,1)S(1)} %compare_and_fusion), kind=kLoop, calls=%fused_computation.6 | loop fusion | flops 393216 | bytes 1573376 | tf_op jit(solution)/shard_map/jit(_take)/select_n | solution.py:44
  26.5 1.5 fusion.26
  28.0 2.6 %copy.59 = bf16[1,8,2,48,512]{3,1,4,2,0:T(8,128)(2,1)S(1)} copy(bf16[1,8,2,48,512]{4,3,2,1,0:T(8,128)(2,1)} %param.12) | data formatting | bytes 1572864 | tf_op args[2]
  30.9 1.5 fusion.27
  32.4 1.5 copy.65
  33.9 0.7 copy.67
  34.7 1.9 %copy.60 = bf16[8,1,48,512]{3,2,0,1:T(8,128)(2,1)S(1)} copy(bf16[8,1,48,512]{2,0,3,1:T(8,128)(2,1)} %get-tuple-element.6) | data formatting | bytes 786432 | tf_op jit(solution)/shard_map/slice | solution.py:48
  39.4 1.1 fusion.8
  40.6 41.1 %all-gather.2.cloned.1.call-done = bf16[1,2,512,512]{3,2,1,0:T(8,128)(2,1)} async-done(((bf16[1,2,32,512]{3,2,1,0:T(8,128)(2,1)}), bf16[1,2,512,512]{3,2,1,0:T(8,128)(2,1)}) %all-gather.2.cloned.1.call-update) | async-done | bytes 1048592 | tf_op jit(solution)/shard_map/all_gather | solution.py:54
  81.7 1.5 fusion.19
  83.2 1.4 fusion.18
  85.6 1.3 fusion.15
  87.0 2.4 %gather_fusion.1 = bf16[32,2,48,512]{3,2,1,0:T(8,128)(2,1)} fusion(bf16[8,2,48,512]{3,2,1,0:T(8,128)(2,1)S(1)} %get-tuple-element.12, s32[1024]{0:T(1024)S(1)} %pad_clamp_fusion.1), kind=kCustom, calls=%fused_computation.1 | custom fusion | bytes 6291584 | tf_op jit(solution)/shard_map/gather | solution.py:81
  89.3 2.4 %gather_fusion.2 = bf16[32,2,48,512]{3,2,1,0:T(8,128)(2,1)} fusion(bf16[8,2,48,512]{3,2,1,0:T(8,128)(2,1)S(1)} %get-tuple-element.7, s32[1024]{0:T(1024)S(1)} %pad_clamp_fusion), kind=kCustom, calls=%fused_computation.2 | custom fusion | bytes 6291584 | tf_op jit(solution)/shard_map/gather | solution.py:82
  91.8 2.6 %fusion = f32[32,48,48]{2,1,0:T(8,128)S(1)} fusion(bf16[32,2,48,512]{3,2,1,0:T(8,128)(2,1)} %gather_fusion.1, bf16[32,2,48,512]{3,2,1,0:T(8,128)(2,1)} %gather_fusion.2), kind=kOutput, calls=%fused_computation.11 | convolution fusion | flops 75497472 | bytes 3440640 | tf_op jit(solution)/shard_map/prb,psb->prs/dot_general | solution.py:17
  94.6 2.1 %fusion.1 = f32[32,48,48]{2,1,0:T(8,128)S(1)} fusion(bf16[32,2,48,512]{3,2,1,0:T(8,128)(2,1)S(1)} %copy-done.5, bf16[32,2,48,512]{3,2,1,0:T(8,128)(2,1)} %gather_fusion.2), kind=kOutput, calls=%fused_computation.12 | convolution fusion | flops 75497472 | bytes 3440640 | tf_op jit(solution)/shard_map/prb,psb->prs/dot_general | solution.py:17
  98.3 1.4 convert_element_type.16
  100.2 50.9 %all_to_all.10 = bf16[32,2,2,2304]{3,2,1,0:T(2,128)(2,1)S(1)} all-to-all(bf16[32,2,2,2304]{3,2,1,0:T(2,128)(2,1)S(1)} %reshape.178), channel_id=1, replica_groups=mesh['grp'=16,'clu'=32] {'clu'}, dimensions={0} | all-to-all | bytes 1179648 | tf_op jit(solution)/shard_map/all_to_all | solution.py:105
  151.0 0.8 copy.80
  (56 shorter events, 7.3 us)
Async XLA Ops:
  9.1 11.1 %copy-start.9 = (s32[1,8]{1,0:T(1,128)S(1)}, s32[1,8]{1,0:T(1,128)}, u32[]{:S(2)}) copy-start(s32[1,8]{1,0:T(1,128)} %param.15) | copy-start | bytes 100
  9.1 11.1 %copy-start.8 = (s32[1,512]{1,0:T(1,128)S(1)}, s32[1,512]{1,0:T(1,128)}, u32[]{:S(2)}) copy-start(s32[1,512]{1,0:T(1,128)} %param.16) | copy-start | bytes 6148
  9.1 28.4 %all-to-all-start = ((bf16[16,1,2,32,512]{4,3,2,1,0:T(8,128)(2,1)}), bf16[16,1,2,32,512]{4,3,2,1,0:T(8,128)(2,1)S(1)}, u32[]{:S(2)}, u32[]{:S(2)}) async-start(bf16[16,1,2,32,512]{4,3,2,1,0:T(8,128)(2,1)} %stack.52), calls=%async_computation | async-start | bytes 2097152 | tf_op jit(solution)/shard_map/all_to_all | solution.py:35
  16.8 64.9 %all-gather.2.cloned.1.call-start = ((), (), s32[]{:S(2)}) async-start(), calls=%async_computation.2 | async-start | bytes 1114112 | tf_op jit(solution)/shard_map/all_gather | solution.py:54
  28.0 2.6 %copy-start.10 = (s32[1,8]{1,0:T(1,128)S(1)}, s32[1,8]{1,0:T(1,128)}, u32[]{:S(2)}) copy-start(s32[1,8]{1,0:T(1,128)} %param.14) | copy-start | bytes 100
  30.8 1.5 copy-start.11
  30.8 1.6 %copy-start.2 = (bf16[8,1,48,512]{2,0,1,3:T(8,128)(2,1)S(1)}, bf16[8,1,48,512]{2,0,1,3:T(8,128)(2,1)}, u32[]{:S(2)}) copy-start(bf16[8,1,48,512]{2,0,1,3:T(8,128)(2,1)} %get-tuple-element.4) | copy-start | bytes 1179652
  30.8 3.1 %copy-start.1 = (bf16[8,1,48,512]{2,0,1,3:T(8,128)(2,1)S(1)}, bf16[8,1,48,512]{2,0,1,3:T(8,128)(2,1)}, u32[]{:S(2)}) copy-start(bf16[8,1,48,512]{2,0,1,3:T(8,128)(2,1)} %get-tuple-element.3) | copy-start | bytes 1179652
  33.9 2.6 %copy-start.3 = (bf16[8,1,48,512]{2,0,3,1:T(8,128)(2,1)S(1)}, bf16[8,1,48,512]{2,0,3,1:T(8,128)(2,1)}, u32[]{:S(2)}) copy-start(bf16[8,1,48,512]{2,0,3,1:T(8,128)(2,1)} %get-tuple-element.5) | copy-start | bytes 1179652
  33.9 3.4 %copy-start.12 = (s32[1,32]{1,0:T(1,128)S(1)}, s32[1,32]{1,0:T(1,128)}, u32[]{:S(2)}) copy-start(s32[1,32]{1,0:T(1,128)} %param.18) | copy-start | bytes 388
  33.9 3.4 %copy-start.13 = (s32[1,32,1]{1,2,0:T(1,128)S(1)}, s32[1,32,1]{1,2,0:T(1,128)}, u32[]{:S(2)}) copy-start(s32[1,32,1]{1,2,0:T(1,128)} %param.19) | copy-start | bytes 388
  37.2 1.0 copy-start.4
  81.7 2.9 %copy-start = (bf16[1,2,512,512]{3,2,1,0:T(8,128)(2,1)S(1)}, bf16[1,2,512,512]{3,2,1,0:T(8,128)(2,1)}, u32[]{:S(2)}) copy-start(bf16[1,2,512,512]{3,2,1,0:T(8,128)(2,1)} %all-gather.2.cloned.1.call-done) | copy-start | bytes 3145732
  84.6 1.0 copy-start.7
  91.8 2.8 %copy-start.5 = (bf16[32,2,48,512]{3,2,1,0:T(8,128)(2,1)S(1)}, bf16[32,2,48,512]{3,2,1,0:T(8,128)(2,1)}, u32[]{:S(2)}) copy-start(bf16[32,2,48,512]{3,2,1,0:T(8,128)(2,1)} %gather_fusion.1) | copy-start | bytes 9437188
  94.6 2.4 %copy-start.6 = (bf16[32,2,48,512]{3,2,1,0:T(8,128)(2,1)S(1)}, bf16[32,2,48,512]{3,2,1,0:T(8,128)(2,1)}, u32[]{:S(2)}) copy-start(bf16[32,2,48,512]{3,2,1,0:T(8,128)(2,1)} %gather_fusion.2) | copy-start | bytes 9437188
Sparse Core Ops, SparseCore 0:
  20.7 60.9 all-gather.1
